TPU v7x, 256 devices: a whole 4x4x8 slice. The times are simulated.
256 devices in a mesh: kv: 8 (over y, z_lo), blk: 32 (over x, z_hi, core).
Axes of the slice: x: 4, y: 4, z: 8 (z_hi: 4, z_lo: 2; z = z_hi * 2 + z_lo), core: 2. Of those that a mesh axis runs over, the one named last changes fastest.
Arguments:
- suffix_query: bfloat16 [6144, 4096], P('blk', 'kv'), may hold values from -6 to 6
- suffix_key_value: bfloat16 [2, 6144, 2048], P(None, 'blk', 'kv'), may hold values from -6 to 6
- suffix_resid: bfloat16 [6144, 4608], P('blk', 'kv'), may hold values from -6 to 6
- decode_query_rows: bfloat16 [64, 4096], P('blk', 'kv'), may hold values from -6 to 6
- decode_key_value: bfloat16 [2, 64, 2048], P(None, 'blk', 'kv'), may hold values from -6 to 6
- decode_resid: bfloat16 [64, 4608], P('blk', 'kv'), may hold values from -6 to 6
- out_weight: bfloat16 [4096, 4608], P('kv'), may hold values from -1.125 to 1.125
- post_gain: float32 [4608], P('kv'), may hold values from 0.1 to 1.9
- prefix_page_store: bfloat16 [2, 96, 128, 2048], P(None, 'blk', None, 'kv'), may hold values from -6 to 6
- prefix_table: int32 [96], replicated, may hold values from 0 to 95, each once
- decode_page_store: bfloat16 [2, 512, 128, 2048], P(None, 'blk', None, 'kv'), may hold values from -6 to 6
- page_table: int32 [512], replicated, may hold values from 0 to 511, each once
- suffix_lengths: int32 [16], replicated, may hold values from 1 to 768, 6144 in all
- suffix_prefix: int32 [16], replicated, may hold values from 0 to 3
- decode_ages: int32 [64], replicated, may hold values from 1 to 1023, as said below
Outputs:
- suffix_hidden: bfloat16 [6144, 4608], P('blk', 'kv')
- decode_hidden: bfloat16 [64, 4608], P('blk', 'kv')
- new_cache: bfloat16 [2, 512, 128, 2048], P(None, 'blk', None, 'kv')
Inputs may be any that keep to these rules, and one draw needn't show every extreme that they name: `page_table`: every page of the decode pool is named once. `prefix_table`: every page of the prefix pool is named once. `suffix_lengths`: the lengths sum to 6144; one is exactly 768. `decode_ages`: some slot has age 1024 - 1.
All inputs are finite; a program needn't handle non-finite values.
Results may differ from a plain program's by a relative error of at most 0.024.
Values may be sent and summed in bfloat16 or wider, within the bound.
No kernel may reach another device: no remote copies, remote signals or barrier semaphores. Data moves between devices by JAX's collectives and lax.ppermute only.
A program may use at most 128 MiB of HBM per device.

v0:
```python
import math
import jax
import jax.numpy as jnp
from jax import lax
from jax.sharding import PartitionSpec as P

D = 4608
QUERY_HEADS = 32
HEAD_SIZE = 128
PAGE_TOKENS = 128
PREFIX_LENGTH = 3072
SLOT_CAPACITY = 1024
soft_cap = 50.0
norm_eps = 1e-06


def from_behind(block, axis, distance):
    devices = range(lax.axis_size(axis))
    route = [(i - distance, i) for i in devices if i - distance in devices]
    return lax.ppermute(block, axis, route)


def attend(query_rows, key_rows, value_rows, visible, q_scale):
    logits = (
        jnp.einsum("qhgd,khd->qhgk", query_rows, key_rows, preferred_element_type=jnp.float32)
        * q_scale
    )
    capped = soft_cap * jnp.tanh(logits / soft_cap)
    weights = jnp.where(visible[:, None, None, :], jnp.exp(capped), 0.0)
    denominator = jnp.sum(weights, axis=3)
    numerator = jnp.einsum(
        "qhgk,khd->qhgd",
        weights.astype(jnp.bfloat16),
        value_rows,
        preferred_element_type=jnp.float32,
    )
    return (numerator, denominator)


def earlier(block_rows):
    return from_behind(block_rows, "blk", 1)


def token_tables(lengths, prefix_ids, token_ids):
    suffix_ends = jnp.cumsum(lengths)
    starts = suffix_ends - lengths
    inside = (
        (token_ids[:, None] >= starts[None, :]) & (token_ids[:, None] < suffix_ends[None, :])
    ).astype(jnp.int32)
    tok_start = jnp.sum(inside * starts[None, :], axis=1)
    tok_prefix = jnp.sum(inside * prefix_ids[None, :], axis=1)
    return (tok_start, tok_prefix)


def inverse_rows(table, wanted):
    hits = (table[None, :] == wanted[:, None]).astype(jnp.int32)
    places = jnp.arange(table.shape[0], dtype=jnp.int32)
    return jnp.sum(hits * places[None, :], axis=1)


def body(
    suffix_query,
    suffix_key_value,
    suffix_resid,
    decode_query_rows,
    decode_key_value,
    decode_resid,
    out_weight,
    post_gain,
    prefix_page_store,
    prefix_table,
    decode_page_store,
    page_table,
    suffix_lengths,
    suffix_prefix,
    decode_ages,
):
    head_dim = HEAD_SIZE
    page_len = PAGE_TOKENS
    q_scale = (D // QUERY_HEADS) ** (-0.5)
    tok_rows = suffix_query.shape[0]
    q_heads = suffix_query.shape[1] // head_dim
    kv_heads = suffix_key_value.shape[2] // head_dim
    query_group_width = q_heads // kv_heads
    my_index = lax.axis_index("blk")
    own_queries = suffix_query.reshape(tok_rows, kv_heads, query_group_width, head_dim)
    token_ids = my_index * tok_rows + jnp.arange(tok_rows, dtype=jnp.int32)
    tok_start, tok_prefix = token_tables(suffix_lengths, suffix_prefix, token_ids)
    look_back = 4
    pieces_back = [suffix_key_value]
    for step in range(look_back):
        pieces_back.insert(0, earlier(pieces_back[0]))
    window = jnp.concatenate(pieces_back, axis=1)
    key_ids = (my_index - look_back) * tok_rows + jnp.arange(
        (look_back + 1) * tok_rows, dtype=jnp.int32
    )
    visible = (key_ids[None, :] >= tok_start[:, None]) & (key_ids[None, :] <= token_ids[:, None])
    window_keys = window[0].reshape((look_back + 1) * tok_rows, kv_heads, head_dim)
    window_values = window[1].reshape((look_back + 1) * tok_rows, kv_heads, head_dim)
    own_numer, own_denom = attend(own_queries, window_keys, window_values, visible, q_scale)
    pool_pages = prefix_table.shape[0]
    page_owner = inverse_rows(prefix_table, jnp.arange(pool_pages, dtype=jnp.int32)) // (
        PREFIX_LENGTH // PAGE_TOKENS
    )
    all_queries = lax.all_gather(suffix_query, "blk", axis=0, tiled=True)
    all_tokens = all_queries.shape[0]
    all_ids = jnp.arange(all_tokens, dtype=jnp.int32)
    unused_start, all_prefix = token_tables(suffix_lengths, suffix_prefix, all_ids)
    local_pages = prefix_page_store.shape[1]
    held_owner = lax.dynamic_slice_in_dim(page_owner, my_index * local_pages, local_pages, 0)
    held_cols = jnp.repeat(held_owner, page_len)
    held_keys = prefix_page_store[0].reshape(local_pages * page_len, kv_heads, head_dim)
    held_values = prefix_page_store[1].reshape(local_pages * page_len, kv_heads, head_dim)
    block_rows = math.gcd(all_tokens, 1024)
    query_blocks = all_queries.reshape(
        all_tokens // block_rows, block_rows, kv_heads, query_group_width, head_dim
    )
    prefix_blocks = all_prefix.reshape(all_tokens // block_rows, block_rows)

    def one_block(element):
        block_queries, block_prefix = element
        seen = block_prefix[:, None] == held_cols[None, :]
        return attend(block_queries, held_keys, held_values, seen, q_scale)

    numer_all, denom_all = lax.map(one_block, (query_blocks, prefix_blocks))
    numer_all = numer_all.reshape(all_tokens, kv_heads, query_group_width, head_dim)
    denom_all = denom_all.reshape(all_tokens, kv_heads, query_group_width)
    pre_numer, pre_denom = (
        lax.psum_scatter(
            numer_all.astype(jnp.bfloat16), "blk", scatter_dimension=0, tiled=True
        ).astype(jnp.float32),
        lax.psum_scatter(
            denom_all.astype(jnp.bfloat16), "blk", scatter_dimension=0, tiled=True
        ).astype(jnp.float32),
    )
    suffix_attn = ((own_numer + pre_numer) / (own_denom + pre_denom)[..., None]).astype(
        jnp.bfloat16
    )
    suffix_attn = suffix_attn.reshape(tok_rows, q_heads * head_dim)
    all_dq, all_dkv = (
        lax.all_gather(decode_query_rows, "blk", axis=0, tiled=True),
        lax.all_gather(decode_key_value, "blk", axis=1, tiled=True),
    )
    slot_total = all_dq.shape[0]
    slot_pages = SLOT_CAPACITY // PAGE_TOKENS
    local_cache = decode_page_store.shape[1]
    page_ids = my_index * local_cache + jnp.arange(local_cache, dtype=jnp.int32)
    position = inverse_rows(page_table, page_ids)
    slot_of = position // slot_pages
    block_of = position % slot_pages
    slot_hot = slot_of[:, None] == jnp.arange(slot_total, dtype=jnp.int32)[None, :]
    page_age = jnp.sum(slot_hot.astype(jnp.int32) * decode_ages[None, :], axis=1)
    select = slot_hot.astype(jnp.bfloat16)
    new_rows = jnp.einsum(
        "ls,tsc->tlc", select, all_dkv, preferred_element_type=jnp.float32
    ).astype(jnp.bfloat16)
    write_here = (block_of == page_age // page_len)[:, None] & (
        jnp.arange(page_len, dtype=jnp.int32)[None, :] == (page_age % page_len)[:, None]
    )
    new_cache = jnp.where(write_here[None, :, :, None], new_rows[:, :, None, :], decode_page_store)
    page_queries = jnp.dot(select, all_dq, preferred_element_type=jnp.float32).astype(jnp.bfloat16)
    page_queries = page_queries.reshape(local_cache, kv_heads, query_group_width, head_dim)
    key_cache = new_cache[0].reshape(local_cache, page_len, kv_heads, head_dim)
    value_cache = new_cache[1].reshape(local_cache, page_len, kv_heads, head_dim)
    logits = (
        jnp.einsum("lhgd,lphd->lhgp", page_queries, key_cache, preferred_element_type=jnp.float32)
        * q_scale
    )
    capped = soft_cap * jnp.tanh(logits / soft_cap)
    places = block_of[:, None] * page_len + jnp.arange(page_len, dtype=jnp.int32)[None, :]
    seen_pos = places <= page_age[:, None]
    weights = jnp.where(seen_pos[:, None, None, :], jnp.exp(capped), 0.0)
    page_denom = jnp.sum(weights, axis=3)
    page_numer = jnp.einsum(
        "lhgp,lphd->lhgd",
        weights.astype(jnp.bfloat16),
        value_cache,
        preferred_element_type=jnp.float32,
    )
    slot_float = slot_hot.astype(jnp.float32)
    slot_numer = jnp.einsum(
        "ls,lhgd->shgd", slot_float, page_numer, precision=lax.Precision.HIGHEST
    )
    slot_denom = jnp.einsum("ls,lhg->shg", slot_float, page_denom, precision=lax.Precision.HIGHEST)
    mine_numer, mine_denom = (
        lax.psum_scatter(
            slot_numer.astype(jnp.bfloat16), "blk", scatter_dimension=0, tiled=True
        ).astype(jnp.float32),
        lax.psum_scatter(
            slot_denom.astype(jnp.bfloat16), "blk", scatter_dimension=0, tiled=True
        ).astype(jnp.float32),
    )
    decode_attn = (mine_numer / mine_denom[..., None]).astype(jnp.bfloat16)
    decode_rows = decode_attn.shape[0]
    decode_attn = decode_attn.reshape(decode_rows, q_heads * head_dim)
    attention = jnp.concatenate([suffix_attn, decode_attn], axis=0)
    projected = jnp.dot(attention, out_weight, preferred_element_type=jnp.float32)
    residual = jnp.concatenate([suffix_resid, decode_resid], axis=0).astype(jnp.float32)
    mine = lax.psum_scatter(
        projected.astype(jnp.bfloat16), "kv", scatter_dimension=1, tiled=True
    ).astype(jnp.float32)
    mean_square = lax.psum(jnp.sum(mine * mine, axis=1), "kv") / D
    normed = mine * lax.rsqrt(mean_square + norm_eps)[:, None] * post_gain[None, :]
    hidden = (residual + normed).astype(jnp.bfloat16)
    return (hidden[:tok_rows], hidden[tok_rows:], new_cache)


def solution(mesh):
    placed = (
        P("blk", "kv"),
        P(None, "blk", "kv"),
        P("blk", "kv"),
        P("blk", "kv"),
        P(None, "blk", "kv"),
        P("blk", "kv"),
        P("kv", None),
        P("kv"),
        P(None, "blk", None, "kv"),
        P(),
        P(None, "blk", None, "kv"),
        P(),
        P(),
        P(),
        P(),
    )
    return jax.shard_map(
        body,
        mesh=mesh,
        in_specs=placed,
        out_specs=(P("blk", "kv"), P("blk", "kv"), P(None, "blk", None, "kv")),
        check_vma=False,
    )
```

profile of v0, /device:TPU:2, one launch (start us, length us, event | category | flops | bytes accessed | tf_op | source)
XLA Modules:
  0.0 656.7 jit_solution(15037850193555876869)
XLA Ops:
  8.7 3.9 copy.90
  12.6 42.1 %all-gather = bf16[32,2,512]{2,1,0:T(2,128)(2,1)S(1)} all-gather(bf16[1,2,512]{2,1,0:T(2,128)(2,1)S(1)} %bitcast.118), channel_id=1, replica_groups=mesh['kv'=8,'blk'=32] {'blk'}, dimensions={0}, use_global_device_ids=true | all-gather | bytes 67584 | tf_op jit(solution)/shard_map/all_gather | solution.py:141
  55.2 42.4 %all_gather.11 = bf16[2,64,256]{2,0,1:T(2,128)(2,1)S(1)} all-gather(bf16[2,2,256]{2,0,1:T(2,128)(2,1)S(1)} %copy.88), channel_id=1, replica_groups=mesh['kv'=8,'blk'=32] {'blk'}, dimensions={1}, use_global_device_ids=true | all-gather | bytes 67584 | tf_op jit(solution)/shard_map/all_gather | solution.py:142
  103.9 9.7 %reshape.292 = bf16[6,1024,2,2,128]{4,3,2,1,0:T(2,128)(2,1)} reshape(bf16[6144,512]{1,0:T(8,128)(2,1)} %all-gather.3.cloned.1.call-done) | data formatting | bytes 12582912 | tf_op jit(solution)/shard_map/reshape | solution.py:115
  113.6 49.5 %while.15 = (s32[]{:T(128)}, bf16[6,1024,2,2,128]{4,1,3,2,0:T(8,128)(2,1)}, bf16[6,1024,2,2]{1,3,2,0:T(2,128)(2,1)S(1)}, s32[6,1024]{1,0:T(8,128)S(1)}, bf16[6,1...) while((s32[]{:T(128)}, ...), condition=%wide.region_6.7_spmd.clone, body=%wide.region_4.6_spmd.clone.sunk | while | flops 818278400 | bytes 19439220 | solution.py:125
  118.6 3.2 bitcast_dynamic-update-slice_fusion.4
  135.1 3.2 bitcast_dynamic-update-slice_fusion.4
  143.3 3.2 bitcast_dynamic-update-slice_fusion.4
  151.6 3.2 bitcast_dynamic-update-slice_fusion.4
  159.8 3.2 bitcast_dynamic-update-slice_fusion.4
  163.1 5.8 copy.117
  168.9 6.3 reshape.304
  175.2 6.1 copy.85
  186.0 125.5 %all-reduce.1 = bf16[64,2,2]{2,0,1:T(8,128)(2,1)S(1)} all-reduce(bf16[64,2,2]{2,0,1:T(8,128)(2,1)S(1)} %convolution_convert_fusion.2), channel_id=5, replica_groups=mesh['kv'=8,'blk'=32] {'blk'}, use_global_device_ids=true, to_apply=%region_14.15.clone | all-reduce | flops 256 | bytes 1024
  313.7 8.1 %collective-permute-done.1 = bf16[2,192,256]{2,1,0:T(8,128)(2,1)S(1)} collective-permute-done((bf16[2,192,256]{2,1,0:T(8,128)(2,1)S(1)}, bf16[2,192,256]{2,1,0:T(8,128)(2,1)S(1)}, u32[]{:S(2)}, u32[]{:S(2)}) %collective-permute-start.1) | collective-permute-done | bytes 196640 | tf_op jit(solution)/shard_map/ppermute | solution.py:20
  323.9 7.8 %collective-permute-done.2 = bf16[2,192,256]{2,1,0:T(8,128)(2,1)S(1)} collective-permute-done((bf16[2,192,256]{2,1,0:T(8,128)(2,1)S(1)}, bf16[2,192,256]{2,1,0:T(8,128)(2,1)S(1)}, u32[]{:S(2)}, u32[]{:S(2)}) %collective-permute-start.2) | collective-permute-done | bytes 196640 | tf_op jit(solution)/shard_map/ppermute | solution.py:20
  333.9 9.5 %all-reduce.4.cloned.1.call-done = bf16[64,2,2,128]{3,0,2,1:T(8,128)(2,1)} async-done(((bf16[64,2,2,128]{3,0,2,1:T(8,128)(2,1)}), bf16[64,2,2,128]{3,0,2,1:T(8,128)(2,1)}) %all-reduce.4.cloned.1.call-update) | async-done | bytes 65552
  345.4 3.9 fusion.10
  349.2 99.7 %reduce-scatter.12.cloned.1.call-done = bf16[192,4]{1,0:T(8,128)(2,1)} async-done(((bf16[6144,4]{1,0:T(8,128)(2,1)}), bf16[192,4]{1,0:T(8,128)(2,1)}) %reduce-scatter.12.cloned.1.call-update) | async-done | bytes 1552
  449.9 109.7 %reduce-scatter.10.cloned.1.call-done = bf16[192,2,2,128]{3,0,2,1:T(8,128)(2,1)} async-done(((bf16[6144,2,2,128]{3,0,2,1:T(8,128)(2,1)}), bf16[192,2,2,128]{3,0,2,1:T(8,128)(2,1)}) %reduce-scatter.10.cloned.1.call-update) | async-done | bytes 196624 | tf_op jit(solution)/shard_map/reduce_scatter | solution.py:129
  562.8 4.7 convolution_convert_fusion
  567.5 4.0 copy.115
  574.2 56.4 %reduce-scatter.14.cloned.1.call-done = bf16[576,194]{1,0:T(8,128)(2,1)} async-done(((bf16[4608,194]{1,0:T(8,128)(2,1)}), bf16[576,194]{1,0:T(8,128)(2,1)}) %reduce-scatter.14.cloned.1.call-update) | async-done | bytes 223504
  631.8 16.9 %psum.7 = f32[194]{0:T(256)S(1)} all-reduce(f32[194]{0:T(256)S(1)} %fusion.32), channel_id=1, replica_groups=mesh['kv'=8,'blk'=32] {'kv'}, use_global_device_ids=true, to_apply=%region_17.18 | all-reduce | flops 194 | bytes 1552 | tf_op jit(solution)/shard_map/psum | solution.py:202
  (146 shorter events, 63.3 us)
Async XLA Ops:
  7.2 5.4 copy-start.6
  7.2 47.6 %copy-start.7 = (s32[512]{0:T(512)S(1)}, s32[512]{0:T(512)}, u32[]{:S(2)}) copy-start(s32[512]{0:T(512)} %param.28) | copy-start | bytes 6148
  7.2 90.3 %copy-start.10 = (s32[64]{0:T(128)S(1)}, s32[64]{0:T(128)}, u32[]{:S(2)}) copy-start(s32[64]{0:T(128)} %param.31) | copy-start | bytes 772
  7.2 96.7 %all-gather.3.cloned.1.call-start = ((), (), s32[]{:S(2)}) async-start(), calls=%async_computation.3 | async-start | bytes 6488064 | tf_op jit(solution)/shard_map/all_gather | solution.py:105
  7.9 335.4 %all-reduce.4.cloned.1.call-start = ((), (), s32[]{:S(2)}) async-start(), calls=%async_computation.7 | async-start | bytes 131072
  100.6 2.4 copy-start.11
  100.6 2.5 copy-start.8
  100.6 2.8 copy-start.9
  100.6 3.0 copy-start.1
  102.9 346.0 %reduce-scatter.12.cloned.1.call-start = ((), (), s32[]{:S(2)}) async-start(), calls=%async_computation.5 | async-start | bytes 1622016
  175.1 384.5 %reduce-scatter.10.cloned.1.call-start = ((), (), s32[]{:S(2)}) async-start(), calls=%async_computation.4 | async-start | bytes 6488064 | tf_op jit(solution)/shard_map/reduce_scatter | solution.py:129
  181.2 0.9 copy-start.3
  181.2 3.2 copy-start
  181.2 3.3 copy-start.12
  181.3 449.3 %reduce-scatter.14.cloned.1.call-start = ((), (), s32[]{:S(2)}) async-start(), calls=%async_computation.6 | async-start | bytes 2654208
  182.2 129.5 %collective-permute-start = (bf16[2,192,256]{2,1,0:T(8,128)(2,1)S(1)}, bf16[2,192,256]{2,1,0:T(8,128)(2,1)S(1)}, u32[]{:S(2)}, u32[]{:S(2)}) collective-permute-start(bf16[2,192,256]{2,1,0:T(8,128)(2,1)S(1)} %copy-done.3), channel_id=1, source_target_pairs={{0,1},{1,2},{2,3},{3,4},{4,5},{5,6},{6,7},{7,8},{8,9},{9,10},{10,1... | collective-permute-start | bytes 589832 | tf_op jit(solution)/shard_map/ppermute | solution.py:20
  311.7 10.1 %collective-permute-start.1 = (bf16[2,192,256]{2,1,0:T(8,128)(2,1)S(1)}, bf16[2,192,256]{2,1,0:T(8,128)(2,1)S(1)}, u32[]{:S(2)}, u32[]{:S(2)}) collective-permute-start(bf16[2,192,256]{2,1,0:T(8,128)(2,1)S(1)} %collective-permute-done), channel_id=1, source_target_pairs={{0,1},{1,2},{2,3},{3,4},{4,5},{5,6},{6,7},{7,8},{8,9},{9,10},{10,1... | collective-permute-start | bytes 589832 | tf_op jit(solution)/shard_map/ppermute | solution.py:20
  321.8 10.0 %collective-permute-start.2 = (bf16[2,192,256]{2,1,0:T(8,128)(2,1)S(1)}, bf16[2,192,256]{2,1,0:T(8,128)(2,1)S(1)}, u32[]{:S(2)}, u32[]{:S(2)}) collective-permute-start(bf16[2,192,256]{2,1,0:T(8,128)(2,1)S(1)} %collective-permute-done.1), channel_id=1, source_target_pairs={{0,1},{1,2},{2,3},{3,4},{4,5},{5,6},{6,7},{7,8},{8,9},{9,10},{10,1... | collective-permute-start | bytes 589832 | tf_op jit(solution)/shard_map/ppermute | solution.py:20
  331.8 12.4 %collective-permute-start.3 = (bf16[2,192,256]{2,1,0:T(8,128)(2,1)S(1)}, bf16[2,192,256]{2,1,0:T(8,128)(2,1)S(1)}, u32[]{:S(2)}, u32[]{:S(2)}) collective-permute-start(bf16[2,192,256]{2,1,0:T(8,128)(2,1)S(1)} %collective-permute-done.2), channel_id=1, source_target_pairs={{0,1},{1,2},{2,3},{3,4},{4,5},{5,6},{6,7},{7,8},{8,9},{9,10},{10,1... | collective-permute-start | bytes 589832 | tf_op jit(solution)/shard_map/ppermute | solution.py:20
  571.5 77.2 %copy-start.2 = (bf16[192,576]{1,0:T(8,128)(2,1)S(1)}, bf16[192,576]{1,0:T(8,128)(2,1)}, u32[]{:S(2)}) copy-start(bf16[192,576]{1,0:T(8,128)(2,1)} %param.19) | copy-start | bytes 663556
  571.5 77.2 %copy-start.4 = (f32[576]{0:T(1024)S(1)}, f32[576]{0:T(1024)}, u32[]{:S(2)}) copy-start(f32[576]{0:T(1024)} %param.24) | copy-start | bytes 6916
  571.6 77.2 %copy-start.5 = (bf16[2,576]{1,0:T(2,128)(2,1)S(1)}, bf16[2,576]{1,0:T(2,128)(2,1)}, u32[]{:S(2)}) copy-start(bf16[2,576]{1,0:T(2,128)(2,1)} %param.22) | copy-start | bytes 6916
Sparse Core Ops, SparseCore 0:
  10.5 72.2 all-gather.2
  103.0 240.3 all-reduce.3
  347.8 101.0 reduce-scatter.11
  452.8 106.7 reduce-scatter.9
  571.7 58.8 reduce-scatter.13
where the time goes:
time: 658 us; the launch traced here: 657 us
  waiting for transfers between devices  292 us (44%)
  blocking collectives  227 us (34%)
  local copies, waits for them, and re-layouts  58.4 us (9%)
  matrix products  49.5 us (8%)
  between operations  14.8 us (2%)
  starting transfers between devices  8.36 us (1%)
  other arithmetic  6.68 us (1%)
    unnamed x8, waiting for transfers between devices  166 us
    unnamed x1, blocking collectives  126 us
    reduce_scatter x1, waiting for transfers between devices, body(): lax.psum_scatter(numer_all.astype(jnp.bfloat16), 'blk', scatter_dimension...  110 us
    all_gather x1, blocking collectives, body(): lax.all_gather(decode_key_value, 'blk', axis=1, tiled=True)  42.4 us
    all_gather x1, blocking collectives, body(): lax.all_gather(decode_query_rows, 'blk', axis=0, tiled=True)  42.1 us
    unnamed x43, local copies, waits for them, and re-layouts  27.1 us
    dot_general x7, matrix products, attend(): jnp.einsum('qhgk,khd->qhgd', weights.astype(jnp.bfloat16), value_rows, pr...  22.1 us
    dot_general x7, matrix products, attend(): jnp.einsum('qhgd,khd->qhgk', query_rows, key_rows, preferred_element_type...  19.9 us
  transfers between devices with their start and end apart: 9, of which 6 were waited for; matrix products, arithmetic and copies ran while one was open for 15% of the time, Pallas kernels for 0%

commit v1 on v0

--- a/solution.py
+++ b/solution.py
@@ -1,3 +1,4 @@
+import functools
 import math
 import jax
 import jax.numpy as jnp
@@ -12,6 +13,13 @@
 SLOT_CAPACITY = 1024
 soft_cap = 50.0
 norm_eps = 1e-06
+
+
+def draft_counts(x_part, comm_axis):
+    return lax.all_gather(x_part, axis_name=comm_axis).sum(axis=0)
+
+
+note_the_lines = functools.partial(draft_counts, comm_axis="kv")
 
 
 def from_behind(block, axis, distance):
@@ -199,7 +207,7 @@
     mine = lax.psum_scatter(
         projected.astype(jnp.bfloat16), "kv", scatter_dimension=1, tiled=True
     ).astype(jnp.float32)
-    mean_square = lax.psum(jnp.sum(mine * mine, axis=1), "kv") / D
+    mean_square = note_the_lines(jnp.sum(mine * mine, axis=1)) / D
     normed = mine * lax.rsqrt(mean_square + norm_eps)[:, None] * post_gain[None, :]
     hidden = (residual + normed).astype(jnp.bfloat16)
     return (hidden[:tok_rows], hidden[tok_rows:], new_cache)

time: 658 us -> 659 us (level)
    unnamed x1 -> x2, blocking collectives: 126 us -> 143 us
    psum x1 -> x0, blocking collectives: 16.9 us -> none  [body(): mean_square = lax.psum(jnp.sum(mine * mine, axis=1), 'kv') / D]
    unnamed x43 -> x48, local copies, waits for them, and re-layouts: 27.1 us -> 27.9 us
where the time goes in v1:
time: 659 us; the launch traced here: 657 us
  waiting for transfers between devices  291 us (44%)
  blocking collectives  227 us (34%)
  local copies, waits for them, and re-layouts  59.4 us (9%)
  matrix products  49.5 us (8%)
  between operations  15.5 us (2%)
  starting transfers between devices  8.35 us (1%)
  other arithmetic  6.7 us (1%)
    unnamed x8, waiting for transfers between devices  165 us
    unnamed x2, blocking collectives  143 us
    reduce_scatter x1, waiting for transfers between devices, body(): lax.psum_scatter(numer_all.astype(jnp.bfloat16), 'blk', scatter_dimension...  110 us
    all_gather x1, blocking collectives, body(): lax.all_gather(decode_key_value, 'blk', axis=1, tiled=True)  42.4 us
    all_gather x1, blocking collectives, body(): lax.all_gather(decode_query_rows, 'blk', axis=0, tiled=True)  42.1 us
    unnamed x48, local copies, waits for them, and re-layouts  27.9 us
    dot_general x7, matrix products, attend(): jnp.einsum('qhgk,khd->qhgd', weights.astype(jnp.bfloat16), value_rows, pr...  22.1 us
    dot_general x7, matrix products, attend(): jnp.einsum('qhgd,khd->qhgk', query_rows, key_rows, preferred_element_type...  19.9 us
  transfers between devices with their start and end apart: 9, of which 6 were waited for; matrix products, arithmetic and copies ran while one was open for 15% of the time, Pallas kernels for 0%

profile of v1, /device:TPU:2, one launch (start us, length us, event | category | flops | bytes accessed | tf_op | source)
XLA Modules:
  0.0 657.4 jit_solution(17358115041359551645)
XLA Ops:
  8.7 3.9 copy.90
  12.6 42.1 %all-gather.1 = bf16[32,2,512]{2,1,0:T(2,128)(2,1)S(1)} all-gather(bf16[1,2,512]{2,1,0:T(2,128)(2,1)S(1)} %bitcast.119), channel_id=1, replica_groups=mesh['kv'=8,'blk'=32] {'blk'}, dimensions={0}, use_global_device_ids=true | all-gather | bytes 67584 | tf_op jit(solution)/shard_map/all_gather | solution.py:149
  55.2 42.4 %all_gather.17 = bf16[2,64,256]{2,0,1:T(2,128)(2,1)S(1)} all-gather(bf16[2,2,256]{2,0,1:T(2,128)(2,1)S(1)} %copy.88), channel_id=1, replica_groups=mesh['kv'=8,'blk'=32] {'blk'}, dimensions={1}, use_global_device_ids=true | all-gather | bytes 67584 | tf_op jit(solution)/shard_map/all_gather | solution.py:150
  103.9 9.7 %reshape.296 = bf16[6,1024,2,2,128]{4,3,2,1,0:T(2,128)(2,1)} reshape(bf16[6144,512]{1,0:T(8,128)(2,1)} %all-gather.4.cloned.1.call-done) | data formatting | bytes 12582912 | tf_op jit(solution)/shard_map/reshape | solution.py:123
  113.6 49.5 %while.15 = (s32[]{:T(128)}, bf16[6,1024,2,2,128]{4,1,3,2,0:T(8,128)(2,1)}, bf16[6,1024,2,2]{1,3,2,0:T(2,128)(2,1)S(1)}, s32[6,1024]{1,0:T(8,128)S(1)}, bf16[6,1...) while((s32[]{:T(128)}, ...), condition=%wide.region_6.7_spmd.clone, body=%wide.region_4.6_spmd.clone.sunk | while | flops 818278400 | bytes 19439220 | solution.py:133
  118.6 3.2 bitcast_dynamic-update-slice_fusion.4
  135.1 3.2 bitcast_dynamic-update-slice_fusion.4
  143.3 3.2 bitcast_dynamic-update-slice_fusion.4
  151.6 3.2 bitcast_dynamic-update-slice_fusion.4
  159.8 3.2 bitcast_dynamic-update-slice_fusion.4
  163.1 5.8 copy.117
  168.9 6.3 reshape.314
  175.2 6.1 copy.85
  186.0 125.4 %all-reduce.2 = bf16[64,2,2]{2,0,1:T(8,128)(2,1)S(1)} all-reduce(bf16[64,2,2]{2,0,1:T(8,128)(2,1)S(1)} %convolution_convert_fusion.2), channel_id=6, replica_groups=mesh['kv'=8,'blk'=32] {'blk'}, use_global_device_ids=true, to_apply=%region_14.15.clone | all-reduce | flops 256 | bytes 1024
  313.6 8.1 %collective-permute-done.1 = bf16[2,192,256]{2,1,0:T(8,128)(2,1)S(1)} collective-permute-done((bf16[2,192,256]{2,1,0:T(8,128)(2,1)S(1)}, bf16[2,192,256]{2,1,0:T(8,128)(2,1)S(1)}, u32[]{:S(2)}, u32[]{:S(2)}) %collective-permute-start.1) | collective-permute-done | bytes 196640 | tf_op jit(solution)/shard_map/ppermute | solution.py:28
  323.9 7.8 %collective-permute-done.2 = bf16[2,192,256]{2,1,0:T(8,128)(2,1)S(1)} collective-permute-done((bf16[2,192,256]{2,1,0:T(8,128)(2,1)S(1)}, bf16[2,192,256]{2,1,0:T(8,128)(2,1)S(1)}, u32[]{:S(2)}, u32[]{:S(2)}) %collective-permute-start.2) | collective-permute-done | bytes 196640 | tf_op jit(solution)/shard_map/ppermute | solution.py:28
  333.8 9.6 %all-reduce.5.cloned.1.call-done = bf16[64,2,2,128]{3,0,2,1:T(8,128)(2,1)} async-done(((bf16[64,2,2,128]{3,0,2,1:T(8,128)(2,1)}), bf16[64,2,2,128]{3,0,2,1:T(8,128)(2,1)}) %all-reduce.5.cloned.1.call-update) | async-done | bytes 65552
  345.4 3.9 fusion.10
  349.3 99.7 %reduce-scatter.12.cloned.1.call-done = bf16[192,4]{1,0:T(8,128)(2,1)} async-done(((bf16[6144,4]{1,0:T(8,128)(2,1)}), bf16[192,4]{1,0:T(8,128)(2,1)}) %reduce-scatter.12.cloned.1.call-update) | async-done | bytes 1552
  449.9 109.7 %reduce-scatter.10.cloned.1.call-done = bf16[192,2,2,128]{3,0,2,1:T(8,128)(2,1)} async-done(((bf16[6144,2,2,128]{3,0,2,1:T(8,128)(2,1)}), bf16[192,2,2,128]{3,0,2,1:T(8,128)(2,1)}) %reduce-scatter.10.cloned.1.call-update) | async-done | bytes 196624 | tf_op jit(solution)/shard_map/reduce_scatter | solution.py:137
  562.8 4.7 convolution_convert_fusion
  567.5 4.0 copy.115
  575.4 55.1 %reduce-scatter.14.cloned.1.call-done = bf16[576,194]{1,0:T(8,128)(2,1)} async-done(((bf16[4608,194]{1,0:T(8,128)(2,1)}), bf16[576,194]{1,0:T(8,128)(2,1)}) %reduce-scatter.14.cloned.1.call-update) | async-done | bytes 223504
  632.1 17.2 %all-reduce = f32[1552]{0:T(1024)S(1)} all-reduce(f32[1552]{0:T(1024)S(1)} %dynamic-update-slice), channel_id=2, replica_groups=mesh['kv'=8,'blk'=32] {'kv'}, use_global_device_ids=true, to_apply=%add | all-reduce | flops 1552 | bytes 12416
  (153 shorter events, 64.3 us)
Async XLA Ops:
  7.2 5.4 copy-start.6
  7.2 47.6 %copy-start.7 = (s32[512]{0:T(512)S(1)}, s32[512]{0:T(512)}, u32[]{:S(2)}) copy-start(s32[512]{0:T(512)} %param.28) | copy-start | bytes 6148
  7.2 90.3 %copy-start.10 = (s32[64]{0:T(128)S(1)}, s32[64]{0:T(128)}, u32[]{:S(2)}) copy-start(s32[64]{0:T(128)} %param.31) | copy-start | bytes 772
  7.2 96.7 %all-gather.4.cloned.1.call-start = ((), (), s32[]{:S(2)}) async-start(), calls=%async_computation.3 | async-start | bytes 6488064 | tf_op jit(solution)/shard_map/all_gather | solution.py:113
  7.9 335.5 %all-reduce.5.cloned.1.call-start = ((), (), s32[]{:S(2)}) async-start(), calls=%async_computation.7 | async-start | bytes 131072
  100.6 2.4 copy-start.11
  100.6 2.5 copy-start.8
  100.6 2.8 copy-start.9
  100.6 3.0 copy-start.1
  102.9 346.0 %reduce-scatter.12.cloned.1.call-start = ((), (), s32[]{:S(2)}) async-start(), calls=%async_computation.5 | async-start | bytes 1622016
  175.2 384.4 %reduce-scatter.10.cloned.1.call-start = ((), (), s32[]{:S(2)}) async-start(), calls=%async_computation.4 | async-start | bytes 6488064 | tf_op jit(solution)/shard_map/reduce_scatter | solution.py:137
  181.3 0.9 copy-start.3
  181.3 3.2 copy-start
  181.3 3.2 copy-start.13
  181.3 449.2 %reduce-scatter.14.cloned.1.call-start = ((), (), s32[]{:S(2)}) async-start(), calls=%async_computation.6 | async-start | bytes 2654208
  182.2 129.4 %collective-permute-start = (bf16[2,192,256]{2,1,0:T(8,128)(2,1)S(1)}, bf16[2,192,256]{2,1,0:T(8,128)(2,1)S(1)}, u32[]{:S(2)}, u32[]{:S(2)}) collective-permute-start(bf16[2,192,256]{2,1,0:T(8,128)(2,1)S(1)} %copy-done.3), channel_id=1, source_target_pairs={{0,1},{1,2},{2,3},{3,4},{4,5},{5,6},{6,7},{7,8},{8,9},{9,10},{10,1... | collective-permute-start | bytes 589832 | tf_op jit(solution)/shard_map/ppermute | solution.py:28
  311.6 10.1 %collective-permute-start.1 = (bf16[2,192,256]{2,1,0:T(8,128)(2,1)S(1)}, bf16[2,192,256]{2,1,0:T(8,128)(2,1)S(1)}, u32[]{:S(2)}, u32[]{:S(2)}) collective-permute-start(bf16[2,192,256]{2,1,0:T(8,128)(2,1)S(1)} %collective-permute-done), channel_id=1, source_target_pairs={{0,1},{1,2},{2,3},{3,4},{4,5},{5,6},{6,7},{7,8},{8,9},{9,10},{10,1... | collective-permute-start | bytes 589832 | tf_op jit(solution)/shard_map/ppermute | solution.py:28
  321.7 10.0 %collective-permute-start.2 = (bf16[2,192,256]{2,1,0:T(8,128)(2,1)S(1)}, bf16[2,192,256]{2,1,0:T(8,128)(2,1)S(1)}, u32[]{:S(2)}, u32[]{:S(2)}) collective-permute-start(bf16[2,192,256]{2,1,0:T(8,128)(2,1)S(1)} %collective-permute-done.1), channel_id=1, source_target_pairs={{0,1},{1,2},{2,3},{3,4},{4,5},{5,6},{6,7},{7,8},{8,9},{9,10},{10,1... | collective-permute-start | bytes 589832 | tf_op jit(solution)/shard_map/ppermute | solution.py:28
  331.7 12.5 %collective-permute-start.3 = (bf16[2,192,256]{2,1,0:T(8,128)(2,1)S(1)}, bf16[2,192,256]{2,1,0:T(8,128)(2,1)S(1)}, u32[]{:S(2)}, u32[]{:S(2)}) collective-permute-start(bf16[2,192,256]{2,1,0:T(8,128)(2,1)S(1)} %collective-permute-done.2), channel_id=1, source_target_pairs={{0,1},{1,2},{2,3},{3,4},{4,5},{5,6},{6,7},{7,8},{8,9},{9,10},{10,1... | collective-permute-start | bytes 589832 | tf_op jit(solution)/shard_map/ppermute | solution.py:28
  571.5 2.6 copy-start.12
  571.5 77.9 %copy-start.2 = (bf16[192,576]{1,0:T(8,128)(2,1)S(1)}, bf16[192,576]{1,0:T(8,128)(2,1)}, u32[]{:S(2)}) copy-start(bf16[192,576]{1,0:T(8,128)(2,1)} %param.19) | copy-start | bytes 663556
  571.5 77.9 %copy-start.4 = (f32[576]{0:T(1024)S(1)}, f32[576]{0:T(1024)}, u32[]{:S(2)}) copy-start(f32[576]{0:T(1024)} %param.24) | copy-start | bytes 6916
  571.5 77.9 %copy-start.5 = (bf16[2,576]{1,0:T(2,128)(2,1)S(1)}, bf16[2,576]{1,0:T(2,128)(2,1)}, u32[]{:S(2)}) copy-start(bf16[2,576]{1,0:T(2,128)(2,1)} %param.22) | copy-start | bytes 6916
Sparse Core Ops, SparseCore 0:
  10.5 72.2 all-gather.3
  103.0 240.3 all-reduce.4
  347.8 101.0 reduce-scatter.11
  452.8 106.7 reduce-scatter.9
  571.7 58.8 reduce-scatter.13
